TPU v7x, 256 devices: a whole 4x4x8 slice. The times are simulated.
256 devices in a mesh: blk: 4 (over y_hi, core), reader: 8 (over y_lo, x), bulk: 8 (over z).
Axes of the slice: x: 4, y: 4 (y_hi: 2, y_lo: 2; y = y_hi * 2 + y_lo), z: 8, core: 2. Of those that a mesh axis runs over, the one named last changes fastest.
Arguments:
- vectors: float32 [128, 32768], P('bulk', ('blk', 'reader')), may hold values from -6 to 6
- ham_tiles: float32 [32, 4, 24, 128, 128], P(('blk', 'reader'))
- tile_rows: int32 [32, 4, 24], P(('blk', 'reader')), may hold values from 0 to 7, as said below
- tile_cols: int32 [32, 4, 24], P(('blk', 'reader')), may hold values from 0 to 63
- center: float32 [1], replicated, may hold values from -0.5 to 0.5
- halfwidth: float32 [1], replicated, may hold values from 1 to 2
Outputs:
- filtered: float32 [128, 32768], P('bulk', ('blk', 'reader'))
Inputs may be any that keep to these rules, and one draw needn't show every extreme that they name: tile_rows and tile_cols of one panel together name 24 different tiles.
All inputs are finite; a program needn't handle non-finite values.
Results may differ from a plain program's by a relative error of at most 0.0003.
Values sent between devices are 32-bit elements; how exact they have to be, the bound alone decides.
No kernel may reach another device: no remote copies, remote signals or barrier semaphores. Data moves between devices by JAX's collectives and lax.ppermute only.
A program may use at most 64 MiB of HBM per device.

v0:
```python
import jax
import jax.numpy as jnp
from jax import lax
from jax.sharding import PartitionSpec as P

TILE = 128
PASSES = 2


def contribute(sources, tiles, rows, count):
    product = jnp.einsum("vkc,krc->vkr", sources, tiles, precision=lax.Precision.HIGHEST)
    onehot = (rows[:, None] == jnp.arange(count, dtype=jnp.int32)[None, :]).astype(jnp.float32)
    return jnp.einsum("vkr,kt->vtr", product, onehot, precision=lax.Precision.HIGHEST)


def apply_ham(current, tiles_here, rows_here, cols_here):
    local_vecs = current.shape[0]
    row_tiles = current.shape[1] // TILE
    groups = tiles_here.shape[0]
    slots = tiles_here.shape[1]
    group_tiles = lax.axis_size("reader") * row_tiles
    whole = lax.all_gather(current, ("blk", "reader"), axis=1, tiled=True)
    tiled = whole.reshape(local_vecs, whole.shape[1] // TILE, TILE)
    offsets = (jnp.arange(groups, dtype=jnp.int32) * group_tiles)[:, None]
    glob = (offsets + cols_here).reshape(-1)
    sources = jnp.take(tiled, glob, axis=1)
    total = contribute(
        sources, tiles_here.reshape(groups * slots, TILE, TILE), rows_here.reshape(-1), row_tiles
    )
    return total.reshape(local_vecs, row_tiles * TILE)


def shards(vectors, ham_tiles, tile_rows, tile_cols, center, halfwidth):
    tiles_here = ham_tiles[0]
    rows_here = tile_rows[0]
    cols_here = tile_cols[0]
    total_rows = vectors.shape[1] * lax.axis_size("blk") * lax.axis_size("reader")

    def scaled(field):
        return (apply_ham(field, tiles_here, rows_here, cols_here) - center[0] * field) / halfwidth[
            0
        ]

    current = vectors
    for step in range(PASSES):
        first = scaled(current)
        second = 2.0 * scaled(first) - current
        third = 2.0 * scaled(second) - first
        squares = lax.psum(jnp.sum(third * third, axis=1), ("blk", "reader"))
        current = third / jnp.sqrt(squares / total_rows + 1e-06)[:, None]
    return current


def solution(mesh):
    return jax.shard_map(
        shards,
        mesh=mesh,
        in_specs=(
            P("bulk", ("blk", "reader")),
            P(("blk", "reader"), None, None, None, None),
            P(("blk", "reader"), None, None),
            P(("blk", "reader"), None, None),
            P(),
            P(),
        ),
        out_specs=P("bulk", ("blk", "reader")),
        check_vma=False,
    )
```

profile of v0, /device:TPU:32, one launch (start us, length us, event | category | flops | bytes accessed | tf_op | source)
XLA Modules:
  0.0 754.0 jit_solution(11329175917317144318)
XLA Ops:
  6.5 0.0 all-gather.7.cloned.1.call-start
  6.5 0.7 all-gather.7.cloned.1.call-update
  7.3 0.0 all-gather.9.cloned.1.call-start
  8.6 0.8 eq.8
  9.4 0.8 squeeze.6
  10.1 0.1 add.20
  10.2 0.1 add.21
  10.3 85.0 %all-gather.7.cloned.1.call-done = f32[16,32768]{1,0:T(8,128)} async-done(((f32[16,1024]{1,0:T(8,128)}), f32[16,32768]{1,0:T(8,128)}) %all-gather.7.cloned.1.call-update) | async-done | bytes 2097168 | tf_op jit(solution)/shard_map/all_gather | solution.py:22
  95.3 1.7 copy_bitcast_fusion.5
  97.1 0.7 gather_fusion
  97.8 0.0 copy-start.2
  97.8 12.0 %convolution_bitcast_fusion.5 = f32[16,96,128]{2,0,1:T(8,128)S(1)} fusion(f32[96,128,128]{2,1,0:T(8,128)} %bitcast.143, f32[96,16,128]{2,1,0:T(8,128)S(1)} %gather_fusion, pred[96]{0:T(512)(128)(4,1)S(1)} %get-tuple-element.10), kind=kOutput, calls=%fused_computation.17 | convolution fusion | flops 302186496 | bytes 7864416 | tf_op jit(solution)/shard_map/vkc,krc->vkr/dot_general | solution.py:11
  109.8 0.6 fusion.16
  110.3 0.0 copy-done.2
  110.3 0.6 fusion.49
  111.0 0.0 all-gather.9.cloned.1.call-update
  111.0 0.0 all-gather.11.cloned.1.call-start
  111.1 85.4 %all-gather.9.cloned.1.call-done = f32[16,32768]{1,0:T(8,128)} async-done(((f32[16,1024]{1,0:T(8,128)}), f32[16,32768]{1,0:T(8,128)}) %all-gather.9.cloned.1.call-update) | async-done | bytes 2097168 | tf_op jit(solution)/shard_map/all_gather | solution.py:22
  196.5 1.7 copy_bitcast_fusion.4
  198.3 0.7 gather_fusion.1
  199.0 0.0 copy-start.1
  199.0 12.0 %convolution_bitcast_fusion.4 = f32[16,96,128]{2,0,1:T(8,128)S(1)} fusion(f32[96,128,128]{2,1,0:T(8,128)} %bitcast.144, f32[96,16,128]{2,1,0:T(8,128)S(1)} %gather_fusion.1, pred[96]{0:T(512)(128)(4,1)S(1)} %get-tuple-element.10), kind=kOutput, calls=%fused_computation.16 | convolution fusion | flops 302186496 | bytes 7864416 | tf_op jit(solution)/shard_map/vkc,krc->vkr/dot_general | solution.py:11
  210.9 0.6 fusion.14
  211.5 0.0 copy-done.1
  211.5 0.7 fusion.48
  212.2 0.0 all-gather.11.cloned.1.call-update
  212.2 0.2 all-gather.13.cloned.1.call-start
  212.4 85.3 %all-gather.11.cloned.1.call-done = f32[16,32768]{1,0:T(8,128)} async-done(((f32[16,1024]{1,0:T(8,128)}), f32[16,32768]{1,0:T(8,128)}) %all-gather.11.cloned.1.call-update) | async-done | bytes 2097168 | tf_op jit(solution)/shard_map/all_gather | solution.py:22
  297.7 1.7 copy_bitcast_fusion.3
  299.4 0.7 gather_fusion.2
  300.1 0.0 copy-start.4
  300.1 12.0 %convolution_bitcast_fusion.3 = f32[16,96,128]{2,0,1:T(8,128)S(1)} fusion(f32[96,128,128]{2,1,0:T(8,128)} %bitcast.145, f32[96,16,128]{2,1,0:T(8,128)S(1)} %gather_fusion.2, pred[96]{0:T(512)(128)(4,1)S(1)} %get-tuple-element.10), kind=kOutput, calls=%fused_computation.15 | convolution fusion | flops 302186496 | bytes 7864416 | tf_op jit(solution)/shard_map/vkc,krc->vkr/dot_general | solution.py:11
  312.1 0.6 fusion.12
  312.7 0.0 copy-done.4
  312.7 0.1 multiply_reduce_fusion.1
  312.8 67.6 %psum.14 = f32[16]{0:T(128)S(1)} all-reduce(f32[16]{0:T(128)S(1)} %get-tuple-element.8), channel_id=1, replica_groups=mesh['blk'=4,'reader'=8,'bulk'=8] {'blk','reader'}, use_global_device_ids=true, to_apply=%region_1.3 | all-reduce | flops 16 | bytes 128 | tf_op jit(solution)/shard_map/psum | solution.py:49
  380.4 0.7 broadcast_divide_fusion.1
  381.1 0.0 all-gather.13.cloned.1.call-update
  381.1 0.0 all-gather.15.cloned.1.call-start
  381.2 80.1 %all-gather.13.cloned.1.call-done = f32[16,32768]{1,0:T(8,128)} async-done(((f32[16,1024]{1,0:T(8,128)}), f32[16,32768]{1,0:T(8,128)}) %all-gather.13.cloned.1.call-update) | async-done | bytes 2097168 | tf_op jit(solution)/shard_map/all_gather | solution.py:22
  461.2 1.7 copy_bitcast_fusion.2
  463.0 0.7 gather_fusion.3
  463.7 11.9 %convolution_bitcast_fusion.2 = f32[16,96,128]{2,0,1:T(8,128)S(1)} fusion(f32[96,128,128]{2,1,0:T(8,128)} %bitcast.146, f32[96,16,128]{2,1,0:T(8,128)S(1)} %gather_fusion.3, pred[96]{0:T(512)(128)(4,1)S(1)} %get-tuple-element.10), kind=kOutput, calls=%fused_computation.14 | convolution fusion | flops 302186496 | bytes 7864416 | tf_op jit(solution)/shard_map/vkc,krc->vkr/dot_general | solution.py:11
  475.6 0.6 fusion.10
  476.2 0.7 fusion.42
  476.9 0.0 all-gather.15.cloned.1.call-update
  476.9 0.3 all-gather.17.cloned.1.call-start
  477.2 85.2 %all-gather.15.cloned.1.call-done = f32[16,32768]{1,0:T(8,128)} async-done(((f32[16,1024]{1,0:T(8,128)}), f32[16,32768]{1,0:T(8,128)}) %all-gather.15.cloned.1.call-update) | async-done | bytes 2097168 | tf_op jit(solution)/shard_map/all_gather | solution.py:22
  562.4 1.7 copy_bitcast_fusion.1
  564.2 0.7 gather_fusion.4
  564.9 0.0 copy-start
  564.9 12.0 %convolution_bitcast_fusion.1 = f32[16,96,128]{2,0,1:T(8,128)S(1)} fusion(f32[96,128,128]{2,1,0:T(8,128)} %bitcast.147, f32[96,16,128]{2,1,0:T(8,128)S(1)} %gather_fusion.4, pred[96]{0:T(512)(128)(4,1)S(1)} %get-tuple-element.10), kind=kOutput, calls=%fused_computation.13 | convolution fusion | flops 302186496 | bytes 7864416 | tf_op jit(solution)/shard_map/vkc,krc->vkr/dot_general | solution.py:11
  576.9 0.6 fusion.8
  577.5 0.7 fusion.41
  578.2 0.0 all-gather.17.cloned.1.call-update
  578.2 85.5 %all-gather.17.cloned.1.call-done = f32[16,32768]{1,0:T(8,128)} async-done(((f32[16,1024]{1,0:T(8,128)}), f32[16,32768]{1,0:T(8,128)}) %all-gather.17.cloned.1.call-update) | async-done | bytes 2097168 | tf_op jit(solution)/shard_map/all_gather | solution.py:22
  663.7 1.7 copy_bitcast_fusion
  665.4 0.7 gather_fusion.5
  666.1 0.0 copy-start.3
  666.1 12.0 %convolution_bitcast_fusion = f32[16,96,128]{2,0,1:T(8,128)S(1)} fusion(f32[96,128,128]{2,1,0:T(8,128)} %bitcast.148, f32[96,16,128]{2,1,0:T(8,128)S(1)} %gather_fusion.5, pred[96]{0:T(512)(128)(4,1)S(1)} %get-tuple-element.10), kind=kOutput, calls=%fused_computation.12 | convolution fusion | flops 302186496 | bytes 7864416 | tf_op jit(solution)/shard_map/vkc,krc->vkr/dot_general | solution.py:11
  678.1 0.6 fusion.6
  678.7 0.1 multiply_reduce_fusion
  678.8 67.6 %psum.15 = f32[16]{0:T(128)S(1)} all-reduce(f32[16]{0:T(128)S(1)} %get-tuple-element.6), channel_id=1, replica_groups=mesh['blk'=4,'reader'=8,'bulk'=8] {'blk','reader'}, use_global_device_ids=true, to_apply=%region_3.5 | all-reduce | flops 16 | bytes 128 | tf_op jit(solution)/shard_map/psum | solution.py:49
  746.4 0.7 broadcast_divide_fusion
  (7 shorter events, 0.0 us)
Async XLA Ops:
  6.5 88.8 %all-gather.7.cloned.1.call-start = ((), (), s32[]{:S(2)}) async-start(), calls=%async_computation | async-start | bytes 2162688 | tf_op jit(solution)/shard_map/all_gather | solution.py:22
  7.3 189.2 %all-gather.9.cloned.1.call-start = ((), (), s32[]{:S(2)}) async-start(), calls=%async_computation.1 | async-start | bytes 2162688 | tf_op jit(solution)/shard_map/all_gather | solution.py:22
  97.8 12.6 %copy-start.2 = (f32[16,1024]{1,0:T(8,128)S(1)}, f32[16,1024]{1,0:T(8,128)}, u32[]{:S(2)}) copy-start(f32[16,1024]{1,0:T(8,128)} %param.8) | copy-start | bytes 196612
  111.0 186.7 %all-gather.11.cloned.1.call-start = ((), (), s32[]{:S(2)}) async-start(), calls=%async_computation.2 | async-start | bytes 2162688 | tf_op jit(solution)/shard_map/all_gather | solution.py:22
  199.0 12.6 %copy-start.1 = (f32[16,1024]{1,0:T(8,128)S(1)}, f32[16,1024]{1,0:T(8,128)}, u32[]{:S(2)}) copy-start(f32[16,1024]{1,0:T(8,128)} %fusion.49) | copy-start | bytes 196612
  212.2 249.0 %all-gather.13.cloned.1.call-start = ((), (), s32[]{:S(2)}) async-start(), calls=%async_computation.3 | async-start | bytes 2162688 | tf_op jit(solution)/shard_map/all_gather | solution.py:22
  300.1 12.6 %copy-start.4 = (f32[16,1024]{1,0:T(8,128)S(1)}, f32[16,1024]{1,0:T(8,128)}, u32[]{:S(2)}) copy-start(f32[16,1024]{1,0:T(8,128)} %fusion.48) | copy-start | bytes 196612
  381.1 181.3 %all-gather.15.cloned.1.call-start = ((), (), s32[]{:S(2)}) async-start(), calls=%async_computation.4 | async-start | bytes 2162688 | tf_op jit(solution)/shard_map/all_gather | solution.py:22
  476.9 186.7 %all-gather.17.cloned.1.call-start = ((), (), s32[]{:S(2)}) async-start(), calls=%async_computation.5 | async-start | bytes 2162688 | tf_op jit(solution)/shard_map/all_gather | solution.py:22
  564.9 12.6 %copy-start = (f32[16,1024]{1,0:T(8,128)S(1)}, f32[16,1024]{1,0:T(8,128)}, u32[]{:S(2)}) copy-start(f32[16,1024]{1,0:T(8,128)} %fusion.42) | copy-start | bytes 196612
  666.1 12.6 %copy-start.3 = (f32[16,1024]{1,0:T(8,128)S(1)}, f32[16,1024]{1,0:T(8,128)}, u32[]{:S(2)}) copy-start(f32[16,1024]{1,0:T(8,128)} %fusion.41) | copy-start | bytes 196612
Sparse Core Ops, SparseCore 0:
  9.1 86.1 all-gather.6
  111.1 85.3 all-gather.8
  212.3 85.3 all-gather.10
  381.3 79.9 all-gather.12
  477.1 85.3 all-gather.14
  578.3 85.3 all-gather.16
where the time goes:
time: 754 us
  waiting for transfers between devices  507 us (67%)
  blocking collectives  135 us (18%)
  matrix products  75.1 us (10%)
  local copies, waits for them, and re-layouts  16.4 us (2%)
  between operations  15 us (2%)
    all_gather x6, waiting for transfers between devices, apply_ham(): whole = lax.all_gather(current, ('blk', 'reader'), axis=1, tiled=True)  506 us
    psum x2, blocking collectives, shards(): squares = lax.psum(jnp.sum(third * third, axis=1), ('blk', 'reader'))  135 us
    dot_general x6, matrix products, contribute(): jnp.einsum('vkc,krc->vkr', sources, tiles, precision=lax.Precision.HIGHEST)  71.7 us
  transfers between devices with their start and end apart: 6, of which 6 were waited for; matrix products, arithmetic and copies ran while one was open for 0% of the time, Pallas kernels for 0%

commit v1 on v0

v1 whole, which is shorter than its diff:
```python
import jax
import jax.numpy as jnp
from jax import lax
from jax.sharding import PartitionSpec as P

TILE = 128
PASSES = 2
AXES = ("blk", "reader")
RING = 4


def device_index(core, y, x):
    return ((y // 2) * 2 + core) * 8 + (y % 2) * 4 + x


def shift_perm(step, first_axis_by_core):
    pairs = []
    for core in range(2):
        axis = first_axis_by_core[core]
        for y in range(RING):
            for x in range(RING):
                if axis == "x":
                    dst = device_index(core, y, (x + step) % RING)
                else:
                    dst = device_index(core, (y + step) % RING, x)
                pairs.append((device_index(core, y, x), dst))
    return pairs


def core_swap_perm():
    pairs = []
    for core in range(2):
        for y in range(RING):
            for x in range(RING):
                pairs.append((device_index(core, y, x), device_index(1 - core, y, x)))
    return pairs


def ring_gather(leaves, axis_by_core):
    plus = shift_perm(1, axis_by_core)
    minus = shift_perm(RING - 1, axis_by_core)
    from_left = lax.ppermute(leaves, AXES, plus)
    from_right = lax.ppermute(leaves, AXES, minus)
    half = leaves[0].shape[0] // 2
    far_a = lax.ppermute([l[:half] for l in from_right], AXES, minus)
    far_b = lax.ppermute([l[half:] for l in from_left], AXES, plus)
    out = []
    for own, r, far0, far1, left in zip(leaves, from_right, far_a, far_b, from_left):
        far = jnp.concatenate([far0, far1], axis=0)
        out.append(jnp.stack([own, r, far, left], axis=0))
    return out


def plane_gather(leaves):
    core = lax.axis_index("blk") % 2
    vecs = leaves[0].shape[0]
    hv = vecs // 2
    mine = [lax.dynamic_slice_in_dim(l, core * hv, hv, axis=0) for l in leaves]
    theirs = [lax.dynamic_slice_in_dim(l, (1 - core) * hv, hv, axis=0) for l in leaves]
    got = lax.ppermute(theirs, AXES, core_swap_perm())
    pair = []
    for m, g in zip(mine, got):
        first = jnp.where(core == 0, m, g)
        second = jnp.where(core == 0, g, m)
        pair.append(jnp.stack([first, second], axis=0))
    stage1 = ring_gather(pair, ("x", "y"))
    stage2 = ring_gather(stage1, ("y", "x"))
    other = lax.ppermute(stage2, AXES, core_swap_perm())
    result = []
    for s, o in zip(stage2, other):
        h0 = jnp.where(core == 0, s, o)
        h1 = jnp.where(core == 0, o, s)
        result.append((h0, h1))
    return result


def layout_index(q_index, x0, y0):
    blk = q_index // 8
    reader = q_index % 8
    cc = blk % 2
    y = (blk // 2) * 2 + reader // 4
    x = reader % 4
    dy = (y - y0) % RING
    dx = (x - x0) % RING
    return (dy * 4 + dx) * 2 + cc, (dx * 4 + dy) * 2 + cc


def butterfly_sum(value):
    def partner(flip):
        pairs = []
        for core in range(2):
            for y in range(RING):
                for x in range(RING):
                    c2, y2, x2 = core, y, x
                    if flip == "core":
                        c2 = 1 - core
                    elif flip == "y1":
                        y2 = y ^ 1
                    elif flip == "y2":
                        y2 = y ^ 2
                    elif flip == "x1":
                        x2 = x ^ 1
                    else:
                        x2 = x ^ 2
                    pairs.append((device_index(core, y, x), device_index(c2, y2, x2)))
        return pairs

    for flip in ("core", "y1", "x1", "y2", "x2"):
        value = value + lax.ppermute(value, AXES, partner(flip))
    return value


def shards(vectors, ham_tiles, tile_rows, tile_cols, center, halfwidth):
    tiles_here = ham_tiles[0]
    rows_here = tile_rows[0]
    cols_here = tile_cols[0]
    vecs = vectors.shape[0]
    hv = vecs // 2
    width = vectors.shape[1]
    row_tiles = width // TILE
    groups = tiles_here.shape[0]
    slots = tiles_here.shape[1]
    nblocks = lax.axis_size("blk") * lax.axis_size("reader")
    total_rows = width * nblocks
    group_tiles = lax.axis_size("reader") * row_tiles

    reader = lax.axis_index("reader")
    blk = lax.axis_index("blk")
    x0 = reader % 4
    y0 = (blk // 2) * 2 + reader // 4

    offsets = (jnp.arange(groups, dtype=jnp.int32) * group_tiles)[:, None]
    glob = (offsets + cols_here).reshape(-1)
    q_of = glob // row_tiles
    t_of = glob % row_tiles
    b0, b1 = layout_index(q_of, x0, y0)
    all_q = jnp.arange(nblocks, dtype=jnp.int32)
    p0, p1 = layout_index(all_q, x0, y0)

    tiles = tiles_here.reshape(groups * slots, TILE, TILE)
    rows = rows_here.reshape(-1)
    onehot = (rows[:, None] == jnp.arange(row_tiles, dtype=jnp.int32)[None, :]).astype(jnp.float32)

    def sources_of(h0, h1):
        f0 = h0.reshape(nblocks, hv, row_tiles, TILE)
        f1 = h1.reshape(nblocks, hv, row_tiles, TILE)
        s0 = f0[b0, :, t_of, :]
        s1 = f1[b1, :, t_of, :]
        return jnp.concatenate([s0, s1], axis=1)

    def apply_sources(sources):
        product = jnp.einsum("kvc,krc->kvr", sources, tiles, precision=lax.Precision.HIGHEST)
        total = jnp.einsum("kvr,kt->vtr", product, onehot, precision=lax.Precision.HIGHEST)
        return total.reshape(vecs, width)

    def scaled(field):
        ((h0, h1),) = plane_gather([field])
        out = apply_sources(sources_of(h0, h1))
        return (out - center[0] * field) / halfwidth[0]

    current = vectors
    third = None
    partial = None
    for step in range(PASSES):
        if step == 0:
            first = scaled(current)
        else:
            (h0, h1), (s0, s1) = plane_gather([third, partial])
            sq0 = s0.reshape(nblocks, hv)[p0]
            sq1 = s1.reshape(nblocks, hv)[p1]
            squares = jnp.sum(jnp.concatenate([sq0, sq1], axis=1), axis=0)
            norm = jnp.sqrt(squares / total_rows + 1e-06)
            current = third / norm[:, None]
            sources = sources_of(h0, h1) / norm[None, :, None]
            first = (apply_sources(sources) - center[0] * current) / halfwidth[0]
        second = 2.0 * scaled(first) - current
        third = 2.0 * scaled(second) - first
        partial = jnp.sum(third * third, axis=1)[:, None]
    squares = butterfly_sum(partial[:, 0])
    return third / jnp.sqrt(squares / total_rows + 1e-06)[:, None]


def solution(mesh):
    return jax.shard_map(
        shards,
        mesh=mesh,
        in_specs=(
            P("bulk", ("blk", "reader")),
            P(("blk", "reader"), None, None, None, None),
            P(("blk", "reader"), None, None),
            P(("blk", "reader"), None, None),
            P(),
            P(),
        ),
        out_specs=P("bulk", ("blk", "reader")),
        check_vma=False,
    )
```

time: 754 us -> 318 us (0.42)
  waiting for transfers between devices: 507 us -> 142 us
  blocking collectives: 135 us -> 0 us
  starting transfers between devices: 0.61 us -> 69 us
  between operations: 15 us -> 2.36 us
    all_gather x6 -> x0, waiting for transfers between devices: 506 us -> none  [apply_ham(): whole = lax.all_gather(current, ('blk', 'reader'), axis=1, tiled=True)]
    ppermute x0 -> x75, waiting for transfers between devices: none -> 142 us  [the longest x14 40.3 us: ring_gather(): from_right = lax.ppermute(leaves, AXES, minus)]
    psum x2 -> x0, blocking collectives: 135 us -> none  [shards(): squares = lax.psum(jnp.sum(third * third, axis=1), ('blk', 'reader'))]
    ppermute x0 -> x75, starting transfers between devices: none -> 69 us  [the longest x14 24.8 us: ring_gather(): far_a = lax.ppermute([l[:half] for l in from_right], AXES, minus)]
    reshape x6 -> x0, local copies, waits for them, and re-layouts: 10.5 us -> none  [apply_ham(): tiled = whole.reshape(local_vecs, whole.shape[1] // TILE, TILE)]
    gather x6 -> x14, local copies, waits for them, and re-layouts: 4.15 us -> 14.4 us  [the longest x6 6.64 us: sources_of(): s1 = f1[b1, :, t_of, :]]
  transfers between devices with their start and end apart: 6 -> 75, of which waited for: 6 -> 63; matrix products, arithmetic and copies ran while one was open for 0% -> 1% of each run, Pallas kernels for 0% -> 0%
where the time goes in v1:
time: 318 us; the launch traced here: 312 us
  waiting for transfers between devices  142 us (45%)
  matrix products  74.5 us (23%)
  starting transfers between devices  69 us (22%)
  local copies, waits for them, and re-layouts  17.2 us (5%)
  other arithmetic  7.18 us (2%)
    dot_general x6, matrix products, apply_sources(): jnp.einsum('kvc,krc->kvr', sources, tiles, precision=lax.Precision.HIGHEST)  71.1 us
    ppermute x14, waiting for transfers between devices, ring_gather(): from_right = lax.ppermute(leaves, AXES, minus)  40.3 us
    ppermute x14, waiting for transfers between devices, ring_gather(): far_b = lax.ppermute([l[half:] for l in from_left], AXES, plus)  36.9 us
    ppermute x14, waiting for transfers between devices, ring_gather(): far_a = lax.ppermute([l[:half] for l in from_right], AXES, minus)  26.6 us
    ppermute x14, starting transfers between devices, ring_gather(): far_a = lax.ppermute([l[:half] for l in from_right], AXES, minus)  24.8 us
    ppermute x14, starting transfers between devices, ring_gather(): from_left = lax.ppermute(leaves, AXES, plus)  22.2 us
    ppermute x5, waiting for transfers between devices, butterfly_sum(): value = value + lax.ppermute(value, AXES, partner(flip))  18.3 us
    ppermute x7, waiting for transfers between devices, plane_gather(): other = lax.ppermute(stage2, AXES, core_swap_perm())  11.7 us
  transfers between devices with their start and end apart: 75, of which 63 were waited for; matrix products, arithmetic and copies ran while one was open for 1% of the time, Pallas kernels for 0%

profile of v1, /device:TPU:32, one launch (start us, length us, event | category | flops | bytes accessed | tf_op | source)
XLA Modules:
  0.0 312.1 jit_solution(4891044692692352865)
XLA Ops:
  2.7 2.8 collective-permute-start.1
  5.6 1.9 collective-permute-done.1
  7.5 3.6 %collective-permute-start.2 = (f32[1,8,1024]{2,1,0:T(8,128)S(1)}, f32[1,8,1024]{2,1,0:T(8,128)S(1)}, u32[]{:S(2)}, u32[]{:S(2)}) collective-permute-start(f32[1,8,1024]{2,1,0:T(8,128)S(1)} %slice.140), channel_id=1, source_target_pairs={{0,24},{8,0},{16,8},{24,16},{32,56},{40,32},{48,40},{56,48},{128,1... | collective-permute-start | bytes 98312 | tf_op jit(solution)/shard_map/ppermute | solution.py:45
  12.7 3.5 %collective-permute-done.4 = f32[1,8,1024]{2,1,0:T(8,128)S(1)} collective-permute-done((f32[1,8,1024]{2,1,0:T(8,128)S(1)}, f32[1,8,1024]{2,1,0:T(8,128)S(1)}, u32[]{:S(2)}, u32[]{:S(2)}) %collective-permute-start.4) | collective-permute-done | bytes 32800 | tf_op jit(solution)/shard_map/ppermute | solution.py:46
  16.3 3.1 collective-permute-start.5
  19.4 3.9 %collective-permute-done.5 = f32[4,2,8,1024]{3,2,1,0:T(8,128)S(1)} collective-permute-done((f32[4,2,8,1024]{3,2,1,0:T(8,128)S(1)}, f32[4,2,8,1024]{3,2,1,0:T(8,128)S(1)}, u32[]{:S(2)}, u32[]{:S(2)}) %collective-permute-start.5) | collective-permute-done | bytes 262176 | tf_op jit(solution)/shard_map/ppermute | solution.py:43
  23.3 3.8 %collective-permute-start.6 = (f32[2,2,8,1024]{3,2,1,0:T(8,128)S(1)}, f32[2,2,8,1024]{3,2,1,0:T(8,128)S(1)}, u32[]{:S(2)}, u32[]{:S(2)}) collective-permute-start(f32[2,2,8,1024]{3,2,1,0:T(8,128)S(1)} %slice.142), channel_id=1, source_target_pairs={{0,160},{8,168},{16,176},{24,184},{32,0},{40,8},{48,16},{56,24},{1... | collective-permute-start | bytes 393224 | tf_op jit(solution)/shard_map/ppermute | solution.py:45
  27.1 2.4 collective-permute-done.6
  29.5 3.8 %collective-permute-done.8 = f32[2,2,8,1024]{3,2,1,0:T(8,128)S(1)} collective-permute-done((f32[2,2,8,1024]{3,2,1,0:T(8,128)S(1)}, f32[2,2,8,1024]{3,2,1,0:T(8,128)S(1)}, u32[]{:S(2)}, u32[]{:S(2)}) %collective-permute-start.8) | collective-permute-done | bytes 131104 | tf_op jit(solution)/shard_map/ppermute | solution.py:46
  40.6 11.8 %fusion = f32[96,16,128]{2,1,0:T(8,128)S(1)} fusion(f32[96,128,128]{2,1,0:T(8,128)} %bitcast.220, f32[96,8,128]{2,1,0:T(8,128)S(1)} %gather_fusion.1, f32[96,8,128]{2,1,0:T(8,128)S(1)} %gather_fusion), kind=kOutput, calls=%fused_computation.20 | convolution fusion | flops 302186496 | bytes 7864320 | tf_op jit(solution)/shard_map/kvc,krc->kvr/dot_general | solution.py:152
  54.6 2.0 collective-permute-start.13
  56.6 2.2 collective-permute-done.11
  60.9 1.9 collective-permute-done.12
  62.8 2.5 collective-permute-done.14
  65.4 2.0 collective-permute-start.17
  67.4 4.3 %collective-permute-done.15 = f32[4,2,8,1024]{3,2,1,0:T(8,128)S(1)} collective-permute-done((f32[4,2,8,1024]{3,2,1,0:T(8,128)S(1)}, f32[4,2,8,1024]{3,2,1,0:T(8,128)S(1)}, u32[]{:S(2)}, u32[]{:S(2)}) %collective-permute-start.15) | collective-permute-done | bytes 262176 | tf_op jit(solution)/shard_map/ppermute | solution.py:43
  74.4 2.4 collective-permute-done.16
  76.8 2.9 collective-permute-done.18
  80.0 2.6 collective-permute-done.19
  85.1 11.8 %fusion.4 = f32[96,16,128]{2,1,0:T(8,128)S(1)} fusion(f32[96,128,128]{2,1,0:T(8,128)} %bitcast.221, f32[96,8,128]{2,1,0:T(8,128)S(1)} %gather_fusion.3, f32[96,8,128]{2,1,0:T(8,128)S(1)} %gather_fusion.2), kind=kOutput, calls=%fused_computation.24 | convolution fusion | flops 302186496 | bytes 7864320 | tf_op jit(solution)/shard_map/kvc,krc->kvr/dot_general | solution.py:152
  98.9 2.0 collective-permute-start.23
  101.0 2.2 collective-permute-done.21
  105.2 1.9 collective-permute-done.22
  107.1 2.5 collective-permute-done.24
  109.8 2.0 collective-permute-start.27
  111.8 4.3 %collective-permute-done.25 = f32[4,2,8,1024]{3,2,1,0:T(8,128)S(1)} collective-permute-done((f32[4,2,8,1024]{3,2,1,0:T(8,128)S(1)}, f32[4,2,8,1024]{3,2,1,0:T(8,128)S(1)}, u32[]{:S(2)}, u32[]{:S(2)}) %collective-permute-start.25) | collective-permute-done | bytes 262176 | tf_op jit(solution)/shard_map/ppermute | solution.py:43
  118.5 2.7 collective-permute-done.26
  121.2 2.7 collective-permute-done.28
  124.1 2.6 collective-permute-done.29
  129.2 11.8 %fusion.8 = f32[96,16,128]{2,1,0:T(8,128)S(1)} fusion(f32[96,128,128]{2,1,0:T(8,128)} %bitcast.222, f32[96,8,128]{2,1,0:T(8,128)S(1)} %gather_fusion.5, f32[96,8,128]{2,1,0:T(8,128)S(1)} %gather_fusion.4), kind=kOutput, calls=%fused_computation.28 | convolution fusion | flops 302186496 | bytes 7864320 | tf_op jit(solution)/shard_map/kvc,krc->kvr/dot_general | solution.py:152
  143.2 2.0 collective-permute-start.33
  145.2 2.2 collective-permute-done.31
  151.3 2.5 collective-permute-done.34
  154.0 2.0 collective-permute-start.37
  157.3 3.0 collective-permute-done.35
  162.8 2.0 collective-permute-start.43
  169.9 2.5 collective-permute-done.44
  172.7 2.5 collective-permute-start.45
  176.5 3.5 %collective-permute-start.46 = (f32[2,2,8,1]{2,1,3,0:T(2,128)S(1)}, f32[2,2,8,1]{2,1,3,0:T(2,128)S(1)}, u32[]{:S(2)}, u32[]{:S(2)}) collective-permute-start(f32[2,2,8,1]{2,1,3,0:T(2,128)S(1)} %slice.158), channel_id=1, source_target_pairs={{0,160},{8,168},{16,176},{24,184},{32,0},{40,8},{48,16},{56,24},{1... | collective-permute-start | bytes 392 | tf_op jit(solution)/shard_map/ppermute | solution.py:45
  181.3 3.5 %collective-permute-done.48 = f32[2,2,8,1]{2,1,3,0:T(2,128)S(1)} collective-permute-done((f32[2,2,8,1]{2,1,3,0:T(2,128)S(1)}, f32[2,2,8,1]{2,1,3,0:T(2,128)S(1)}, u32[]{:S(2)}, u32[]{:S(2)}) %collective-permute-start.48) | collective-permute-done | bytes 160 | tf_op jit(solution)/shard_map/ppermute | solution.py:46
  191.5 11.9 %fusion.12 = f32[96,16,128]{2,1,0:T(8,128)S(1)} fusion(f32[96,128,128]{2,1,0:T(8,128)} %bitcast.223, f32[96,8,128]{2,1,0:T(8,128)S(1)} %gather_fusion.7, f32[96,8,128]{2,1,0:T(8,128)S(1)} %gather_fusion.6, f32[16]{0:T(128)S(1)} %add_sqrt_fusion.1), kind=kOutput, calls=%fused_computation.33 | convolution fusion | flops 302383104 | bytes 7864384 | tf_op jit(solution)/shard_map/kvc,krc->kvr/dot_general | solution.py:152
  205.6 2.0 collective-permute-start.53
  207.6 2.2 collective-permute-done.51
  211.9 1.9 collective-permute-done.52
  213.7 2.5 collective-permute-done.54
  216.4 2.0 collective-permute-start.57
  218.4 4.3 %collective-permute-done.55 = f32[4,2,8,1024]{3,2,1,0:T(8,128)S(1)} collective-permute-done((f32[4,2,8,1024]{3,2,1,0:T(8,128)S(1)}, f32[4,2,8,1024]{3,2,1,0:T(8,128)S(1)}, u32[]{:S(2)}, u32[]{:S(2)}) %collective-permute-start.55) | collective-permute-done | bytes 262176 | tf_op jit(solution)/shard_map/ppermute | solution.py:43
  225.1 2.7 collective-permute-done.56
  227.8 2.7 collective-permute-done.58
  230.7 2.6 collective-permute-done.59
  235.8 11.8 %fusion.15 = f32[96,16,128]{2,1,0:T(8,128)S(1)} fusion(f32[96,128,128]{2,1,0:T(8,128)} %bitcast.224, f32[96,8,128]{2,1,0:T(8,128)S(1)} %gather_fusion.11, f32[96,8,128]{2,1,0:T(8,128)S(1)} %gather_fusion.10), kind=kOutput, calls=%fused_computation.36 | convolution fusion | flops 302186496 | bytes 7864320 | tf_op jit(solution)/shard_map/kvc,krc->kvr/dot_general | solution.py:152
  249.7 2.0 collective-permute-start.63
  251.8 2.2 collective-permute-done.61
  257.9 2.5 collective-permute-done.64
  260.6 2.0 collective-permute-start.67
  262.6 4.3 %collective-permute-done.65 = f32[4,2,8,1024]{3,2,1,0:T(8,128)S(1)} collective-permute-done((f32[4,2,8,1024]{3,2,1,0:T(8,128)S(1)}, f32[4,2,8,1024]{3,2,1,0:T(8,128)S(1)}, u32[]{:S(2)}, u32[]{:S(2)}) %collective-permute-start.65) | collective-permute-done | bytes 262176 | tf_op jit(solution)/shard_map/ppermute | solution.py:43
  269.4 2.6 collective-permute-done.66
  272.0 2.7 collective-permute-done.68
  274.9 2.6 collective-permute-done.69
  280.0 11.8 %fusion.19 = f32[96,16,128]{2,1,0:T(8,128)S(1)} fusion(f32[96,128,128]{2,1,0:T(8,128)} %bitcast.225, f32[96,8,128]{2,1,0:T(8,128)S(1)} %gather_fusion.13, f32[96,8,128]{2,1,0:T(8,128)S(1)} %gather_fusion.12), kind=kOutput, calls=%fused_computation.40 | convolution fusion | flops 302186496 | bytes 7864320 | tf_op jit(solution)/shard_map/kvc,krc->kvr/dot_general | solution.py:152
  293.8 3.6 %collective-permute-done.71 = f32[16]{0:T(128)S(1)} collective-permute-done((f32[16]{0:T(128)S(1)}, f32[16]{0:T(128)S(1)}, u32[]{:S(2)}, u32[]{:S(2)}) %collective-permute-start.71) | collective-permute-done | bytes 96 | tf_op jit(solution)/shard_map/ppermute | solution.py:109
  297.4 3.6 %collective-permute-done.72 = f32[16]{0:T(128)S(1)} collective-permute-done((f32[16]{0:T(128)S(1)}, f32[16]{0:T(128)S(1)}, u32[]{:S(2)}, u32[]{:S(2)}) %collective-permute-start.72) | collective-permute-done | bytes 96 | tf_op jit(solution)/shard_map/ppermute | solution.py:109
  301.0 5.1 %collective-permute-done.73 = f32[16]{0:T(128)S(1)} collective-permute-done((f32[16]{0:T(128)S(1)}, f32[16]{0:T(128)S(1)}, u32[]{:S(2)}, u32[]{:S(2)}) %collective-permute-start.73) | collective-permute-done | bytes 96 | tf_op jit(solution)/shard_map/ppermute | solution.py:109
  306.0 5.1 %collective-permute-done.74 = f32[16]{0:T(128)S(1)} collective-permute-done((f32[16]{0:T(128)S(1)}, f32[16]{0:T(128)S(1)}, u32[]{:S(2)}, u32[]{:S(2)}) %collective-permute-start.74) | collective-permute-done | bytes 96 | tf_op jit(solution)/shard_map/ppermute | solution.py:109
  (224 shorter events, 76.6 us)
Async XLA Ops:
  2.7 4.7 %collective-permute-start.1 = (f32[2,8,1024]{2,1,0:T(8,128)S(1)}, f32[2,8,1024]{2,1,0:T(8,128)S(1)}, u32[]{:S(2)}, u32[]{:S(2)}) collective-permute-start(f32[2,8,1024]{2,1,0:T(8,128)S(1)} %get-tuple-element.64), channel_id=1, source_target_pairs={{0,24},{8,0},{16,8},{24,16},{32,56},{40,32},{48,40},{56,48},{128,1... | collective-permute-start | bytes 196616 | tf_op jit(solution)/shard_map/ppermute | solution.py:43
  5.6 5.5 %collective-permute-start.3 = (f32[2,8,1024]{2,1,0:T(8,128)S(1)}, f32[2,8,1024]{2,1,0:T(8,128)S(1)}, u32[]{:S(2)}, u32[]{:S(2)}) collective-permute-start(f32[2,8,1024]{2,1,0:T(8,128)S(1)} %get-tuple-element.64), channel_id=1, source_target_pairs={{0,8},{8,16},{16,24},{24,0},{32,40},{40,48},{48,56},{56,32},{128,1... | collective-permute-start | bytes 196616 | tf_op jit(solution)/shard_map/ppermute | solution.py:42
  7.5 5.2 %collective-permute-start.2 = (f32[1,8,1024]{2,1,0:T(8,128)S(1)}, f32[1,8,1024]{2,1,0:T(8,128)S(1)}, u32[]{:S(2)}, u32[]{:S(2)}) collective-permute-start(f32[1,8,1024]{2,1,0:T(8,128)S(1)} %slice.140), channel_id=1, source_target_pairs={{0,24},{8,0},{16,8},{24,16},{32,56},{40,32},{48,40},{56,48},{128,1... | collective-permute-start | bytes 98312 | tf_op jit(solution)/shard_map/ppermute | solution.py:45
  11.1 5.1 %collective-permute-start.4 = (f32[1,8,1024]{2,1,0:T(8,128)S(1)}, f32[1,8,1024]{2,1,0:T(8,128)S(1)}, u32[]{:S(2)}, u32[]{:S(2)}) collective-permute-start(f32[1,8,1024]{2,1,0:T(8,128)S(1)} %slice.141), channel_id=1, source_target_pairs={{0,8},{8,16},{16,24},{24,0},{32,40},{40,48},{48,56},{56,32},{128,1... | collective-permute-start | bytes 98312 | tf_op jit(solution)/shard_map/ppermute | solution.py:46
  16.3 7.0 %collective-permute-start.5 = (f32[4,2,8,1024]{3,2,1,0:T(8,128)S(1)}, f32[4,2,8,1024]{3,2,1,0:T(8,128)S(1)}, u32[]{:S(2)}, u32[]{:S(2)}) collective-permute-start(f32[4,2,8,1024]{3,2,1,0:T(8,128)S(1)} %get-tuple-element.40), channel_id=1, source_target_pairs={{0,160},{8,168},{16,176},{24,184},{32,0},{40,8},{48,16},{56,24},{1... | collective-permute-start | bytes 786440 | tf_op jit(solution)/shard_map/ppermute | solution.py:43
  19.3 7.7 %collective-permute-start.7 = (f32[4,2,8,1024]{3,2,1,0:T(8,128)S(1)}, f32[4,2,8,1024]{3,2,1,0:T(8,128)S(1)}, u32[]{:S(2)}, u32[]{:S(2)}) collective-permute-start(f32[4,2,8,1024]{3,2,1,0:T(8,128)S(1)} %get-tuple-element.40), channel_id=1, source_target_pairs={{0,32},{8,40},{16,48},{24,56},{32,128},{40,136},{48,144},{56,152},... | collective-permute-start | bytes 786440 | tf_op jit(solution)/shard_map/ppermute | solution.py:42
  23.3 6.3 %collective-permute-start.6 = (f32[2,2,8,1024]{3,2,1,0:T(8,128)S(1)}, f32[2,2,8,1024]{3,2,1,0:T(8,128)S(1)}, u32[]{:S(2)}, u32[]{:S(2)}) collective-permute-start(f32[2,2,8,1024]{3,2,1,0:T(8,128)S(1)} %slice.142), channel_id=1, source_target_pairs={{0,160},{8,168},{16,176},{24,184},{32,0},{40,8},{48,16},{56,24},{1... | collective-permute-start | bytes 393224 | tf_op jit(solution)/shard_map/ppermute | solution.py:45
  27.0 6.3 %collective-permute-start.8 = (f32[2,2,8,1024]{3,2,1,0:T(8,128)S(1)}, f32[2,2,8,1024]{3,2,1,0:T(8,128)S(1)}, u32[]{:S(2)}, u32[]{:S(2)}) collective-permute-start(f32[2,2,8,1024]{3,2,1,0:T(8,128)S(1)} %slice.143), channel_id=1, source_target_pairs={{0,32},{8,40},{16,48},{24,56},{32,128},{40,136},{48,144},{56,152},... | collective-permute-start | bytes 393224 | tf_op jit(solution)/shard_map/ppermute | solution.py:46
  33.4 3.4 %collective-permute-start.9 = (f32[4,4,2,8,1024]{4,3,2,1,0:T(8,128)S(1)}, f32[4,4,2,8,1024]{4,3,2,1,0:T(8,128)}, u32[]{:S(2)}, u32[]{:S(2)}) collective-permute-start(f32[4,4,2,8,1024]{4,3,2,1,0:T(8,128)S(1)} %pad_maximum_fusion), channel_id=1, source_target_pairs={{0,64},{8,72},{16,80},{24,88},{32,96},{40,104},{48,112},{56,120},{... | collective-permute-start | bytes 3145736 | tf_op jit(solution)/shard_map/ppermute | solution.py:68
  54.5 4.3 %collective-permute-start.11 = (f32[2,8,1024]{2,1,0:T(8,128)S(1)}, f32[2,8,1024]{2,1,0:T(8,128)S(1)}, u32[]{:S(2)}, u32[]{:S(2)}) collective-permute-start(f32[2,8,1024]{2,1,0:T(8,128)S(1)} %get-tuple-element.62), channel_id=1, source_target_pairs={{0,24},{8,0},{16,8},{24,16},{32,56},{40,32},{48,40},{56,48},{128,1... | collective-permute-start | bytes 196616 | tf_op jit(solution)/shard_map/ppermute | solution.py:43
  54.6 5.6 %collective-permute-start.13 = (f32[2,8,1024]{2,1,0:T(8,128)S(1)}, f32[2,8,1024]{2,1,0:T(8,128)S(1)}, u32[]{:S(2)}, u32[]{:S(2)}) collective-permute-start(f32[2,8,1024]{2,1,0:T(8,128)S(1)} %get-tuple-element.62), channel_id=1, source_target_pairs={{0,8},{8,16},{16,24},{24,0},{32,40},{40,48},{48,56},{56,32},{128,1... | collective-permute-start | bytes 196616 | tf_op jit(solution)/shard_map/ppermute | solution.py:42
  58.9 3.9 %collective-permute-start.12 = (f32[1,8,1024]{2,1,0:T(8,128)S(1)}, f32[1,8,1024]{2,1,0:T(8,128)S(1)}, u32[]{:S(2)}, u32[]{:S(2)}) collective-permute-start(f32[1,8,1024]{2,1,0:T(8,128)S(1)} %slice.144), channel_id=1, source_target_pairs={{0,24},{8,0},{16,8},{24,16},{32,56},{40,32},{48,40},{56,48},{128,1... | collective-permute-start | bytes 98312 | tf_op jit(solution)/shard_map/ppermute | solution.py:45
  60.2 5.1 %collective-permute-start.14 = (f32[1,8,1024]{2,1,0:T(8,128)S(1)}, f32[1,8,1024]{2,1,0:T(8,128)S(1)}, u32[]{:S(2)}, u32[]{:S(2)}) collective-permute-start(f32[1,8,1024]{2,1,0:T(8,128)S(1)} %slice.145), channel_id=1, source_target_pairs={{0,8},{8,16},{16,24},{24,0},{32,40},{40,48},{48,56},{56,32},{128,1... | collective-permute-start | bytes 98312 | tf_op jit(solution)/shard_map/ppermute | solution.py:46
  65.3 6.4 %collective-permute-start.15 = (f32[4,2,8,1024]{3,2,1,0:T(8,128)S(1)}, f32[4,2,8,1024]{3,2,1,0:T(8,128)S(1)}, u32[]{:S(2)}, u32[]{:S(2)}) collective-permute-start(f32[4,2,8,1024]{3,2,1,0:T(8,128)S(1)} %get-tuple-element.38), channel_id=1, source_target_pairs={{0,160},{8,168},{16,176},{24,184},{32,0},{40,8},{48,16},{56,24},{1... | collective-permute-start | bytes 786440 | tf_op jit(solution)/shard_map/ppermute | solution.py:43
  65.4 7.7 %collective-permute-start.17 = (f32[4,2,8,1024]{3,2,1,0:T(8,128)S(1)}, f32[4,2,8,1024]{3,2,1,0:T(8,128)S(1)}, u32[]{:S(2)}, u32[]{:S(2)}) collective-permute-start(f32[4,2,8,1024]{3,2,1,0:T(8,128)S(1)} %get-tuple-element.38), channel_id=1, source_target_pairs={{0,32},{8,40},{16,48},{24,56},{32,128},{40,136},{48,144},{56,152},... | collective-permute-start | bytes 786440 | tf_op jit(solution)/shard_map/ppermute | solution.py:42
  71.8 5.0 %collective-permute-start.16 = (f32[2,2,8,1024]{3,2,1,0:T(8,128)S(1)}, f32[2,2,8,1024]{3,2,1,0:T(8,128)S(1)}, u32[]{:S(2)}, u32[]{:S(2)}) collective-permute-start(f32[2,2,8,1024]{3,2,1,0:T(8,128)S(1)} %slice.146), channel_id=1, source_target_pairs={{0,160},{8,168},{16,176},{24,184},{32,0},{40,8},{48,16},{56,24},{1... | collective-permute-start | bytes 393224 | tf_op jit(solution)/shard_map/ppermute | solution.py:45
  73.1 6.7 %collective-permute-start.18 = (f32[2,2,8,1024]{3,2,1,0:T(8,128)S(1)}, f32[2,2,8,1024]{3,2,1,0:T(8,128)S(1)}, u32[]{:S(2)}, u32[]{:S(2)}) collective-permute-start(f32[2,2,8,1024]{3,2,1,0:T(8,128)S(1)} %slice.147), channel_id=1, source_target_pairs={{0,32},{8,40},{16,48},{24,56},{32,128},{40,136},{48,144},{56,152},... | collective-permute-start | bytes 393224 | tf_op jit(solution)/shard_map/ppermute | solution.py:46
  98.9 4.3 %collective-permute-start.21 = (f32[2,8,1024]{2,1,0:T(8,128)S(1)}, f32[2,8,1024]{2,1,0:T(8,128)S(1)}, u32[]{:S(2)}, u32[]{:S(2)}) collective-permute-start(f32[2,8,1024]{2,1,0:T(8,128)S(1)} %get-tuple-element.60), channel_id=1, source_target_pairs={{0,24},{8,0},{16,8},{24,16},{32,56},{40,32},{48,40},{56,48},{128,1... | collective-permute-start | bytes 196616 | tf_op jit(solution)/shard_map/ppermute | solution.py:43
  98.9 5.6 %collective-permute-start.23 = (f32[2,8,1024]{2,1,0:T(8,128)S(1)}, f32[2,8,1024]{2,1,0:T(8,128)S(1)}, u32[]{:S(2)}, u32[]{:S(2)}) collective-permute-start(f32[2,8,1024]{2,1,0:T(8,128)S(1)} %get-tuple-element.60), channel_id=1, source_target_pairs={{0,8},{8,16},{16,24},{24,0},{32,40},{40,48},{48,56},{56,32},{128,1... | collective-permute-start | bytes 196616 | tf_op jit(solution)/shard_map/ppermute | solution.py:42
  103.2 3.9 %collective-permute-start.22 = (f32[1,8,1024]{2,1,0:T(8,128)S(1)}, f32[1,8,1024]{2,1,0:T(8,128)S(1)}, u32[]{:S(2)}, u32[]{:S(2)}) collective-permute-start(f32[1,8,1024]{2,1,0:T(8,128)S(1)} %slice.148), channel_id=1, source_target_pairs={{0,24},{8,0},{16,8},{24,16},{32,56},{40,32},{48,40},{56,48},{128,1... | collective-permute-start | bytes 98312 | tf_op jit(solution)/shard_map/ppermute | solution.py:45
  104.5 5.1 %collective-permute-start.24 = (f32[1,8,1024]{2,1,0:T(8,128)S(1)}, f32[1,8,1024]{2,1,0:T(8,128)S(1)}, u32[]{:S(2)}, u32[]{:S(2)}) collective-permute-start(f32[1,8,1024]{2,1,0:T(8,128)S(1)} %slice.149), channel_id=1, source_target_pairs={{0,8},{8,16},{16,24},{24,0},{32,40},{40,48},{48,56},{56,32},{128,1... | collective-permute-start | bytes 98312 | tf_op jit(solution)/shard_map/ppermute | solution.py:46
  109.7 6.4 %collective-permute-start.25 = (f32[4,2,8,1024]{3,2,1,0:T(8,128)S(1)}, f32[4,2,8,1024]{3,2,1,0:T(8,128)S(1)}, u32[]{:S(2)}, u32[]{:S(2)}) collective-permute-start(f32[4,2,8,1024]{3,2,1,0:T(8,128)S(1)} %get-tuple-element.36), channel_id=1, source_target_pairs={{0,160},{8,168},{16,176},{24,184},{32,0},{40,8},{48,16},{56,24},{1... | collective-permute-start | bytes 786440 | tf_op jit(solution)/shard_map/ppermute | solution.py:43
  109.8 7.7 %collective-permute-start.27 = (f32[4,2,8,1024]{3,2,1,0:T(8,128)S(1)}, f32[4,2,8,1024]{3,2,1,0:T(8,128)S(1)}, u32[]{:S(2)}, u32[]{:S(2)}) collective-permute-start(f32[4,2,8,1024]{3,2,1,0:T(8,128)S(1)} %get-tuple-element.36), channel_id=1, source_target_pairs={{0,32},{8,40},{16,48},{24,56},{32,128},{40,136},{48,144},{56,152},... | collective-permute-start | bytes 786440 | tf_op jit(solution)/shard_map/ppermute | solution.py:42
  116.2 5.0 %collective-permute-start.26 = (f32[2,2,8,1024]{3,2,1,0:T(8,128)S(1)}, f32[2,2,8,1024]{3,2,1,0:T(8,128)S(1)}, u32[]{:S(2)}, u32[]{:S(2)}) collective-permute-start(f32[2,2,8,1024]{3,2,1,0:T(8,128)S(1)} %slice.150), channel_id=1, source_target_pairs={{0,160},{8,168},{16,176},{24,184},{32,0},{40,8},{48,16},{56,24},{1... | collective-permute-start | bytes 393224 | tf_op jit(solution)/shard_map/ppermute | solution.py:45
  117.5 6.4 %collective-permute-start.28 = (f32[2,2,8,1024]{3,2,1,0:T(8,128)S(1)}, f32[2,2,8,1024]{3,2,1,0:T(8,128)S(1)}, u32[]{:S(2)}, u32[]{:S(2)}) collective-permute-start(f32[2,2,8,1024]{3,2,1,0:T(8,128)S(1)} %slice.151), channel_id=1, source_target_pairs={{0,32},{8,40},{16,48},{24,56},{32,128},{40,136},{48,144},{56,152},... | collective-permute-start | bytes 393224 | tf_op jit(solution)/shard_map/ppermute | solution.py:46
  143.1 4.3 %collective-permute-start.31 = (f32[2,8,1024]{2,1,0:T(8,128)S(1)}, f32[2,8,1024]{2,1,0:T(8,128)S(1)}, u32[]{:S(2)}, u32[]{:S(2)}) collective-permute-start(f32[2,8,1024]{2,1,0:T(8,128)S(1)} %get-tuple-element.58), channel_id=1, source_target_pairs={{0,24},{8,0},{16,8},{24,16},{32,56},{40,32},{48,40},{56,48},{128,1... | collective-permute-start | bytes 196616 | tf_op jit(solution)/shard_map/ppermute | solution.py:43
  143.2 5.6 %collective-permute-start.33 = (f32[2,8,1024]{2,1,0:T(8,128)S(1)}, f32[2,8,1024]{2,1,0:T(8,128)S(1)}, u32[]{:S(2)}, u32[]{:S(2)}) collective-permute-start(f32[2,8,1024]{2,1,0:T(8,128)S(1)} %get-tuple-element.58), channel_id=1, source_target_pairs={{0,8},{8,16},{16,24},{24,0},{32,40},{40,48},{48,56},{56,32},{128,1... | collective-permute-start | bytes 196616 | tf_op jit(solution)/shard_map/ppermute | solution.py:42
  147.4 3.9 %collective-permute-start.32 = (f32[1,8,1024]{2,1,0:T(8,128)S(1)}, f32[1,8,1024]{2,1,0:T(8,128)S(1)}, u32[]{:S(2)}, u32[]{:S(2)}) collective-permute-start(f32[1,8,1024]{2,1,0:T(8,128)S(1)} %slice.152), channel_id=1, source_target_pairs={{0,24},{8,0},{16,8},{24,16},{32,56},{40,32},{48,40},{56,48},{128,1... | collective-permute-start | bytes 98312 | tf_op jit(solution)/shard_map/ppermute | solution.py:45
  148.7 5.1 %collective-permute-start.34 = (f32[1,8,1024]{2,1,0:T(8,128)S(1)}, f32[1,8,1024]{2,1,0:T(8,128)S(1)}, u32[]{:S(2)}, u32[]{:S(2)}) collective-permute-start(f32[1,8,1024]{2,1,0:T(8,128)S(1)} %slice.153), channel_id=1, source_target_pairs={{0,8},{8,16},{16,24},{24,0},{32,40},{40,48},{48,56},{56,32},{128,1... | collective-permute-start | bytes 98312 | tf_op jit(solution)/shard_map/ppermute | solution.py:46
  153.9 6.4 %collective-permute-start.35 = (f32[4,2,8,1024]{3,2,1,0:T(8,128)S(1)}, f32[4,2,8,1024]{3,2,1,0:T(8,128)S(1)}, u32[]{:S(2)}, u32[]{:S(2)}) collective-permute-start(f32[4,2,8,1024]{3,2,1,0:T(8,128)S(1)} %get-tuple-element.34), channel_id=1, source_target_pairs={{0,160},{8,168},{16,176},{24,184},{32,0},{40,8},{48,16},{56,24},{1... | collective-permute-start | bytes 786440 | tf_op jit(solution)/shard_map/ppermute | solution.py:43
  154.0 7.9 %collective-permute-start.37 = (f32[4,2,8,1024]{3,2,1,0:T(8,128)S(1)}, f32[4,2,8,1024]{3,2,1,0:T(8,128)S(1)}, u32[]{:S(2)}, u32[]{:S(2)}) collective-permute-start(f32[4,2,8,1024]{3,2,1,0:T(8,128)S(1)} %get-tuple-element.34), channel_id=1, source_target_pairs={{0,32},{8,40},{16,48},{24,56},{32,128},{40,136},{48,144},{56,152},... | collective-permute-start | bytes 786440 | tf_op jit(solution)/shard_map/ppermute | solution.py:42
  160.4 12.1 %collective-permute-start.36 = (f32[2,2,8,1024]{3,2,1,0:T(8,128)S(1)}, f32[2,2,8,1024]{3,2,1,0:T(8,128)S(1)}, u32[]{:S(2)}, u32[]{:S(2)}) collective-permute-start(f32[2,2,8,1024]{3,2,1,0:T(8,128)S(1)} %slice.154), channel_id=1, source_target_pairs={{0,160},{8,168},{16,176},{24,184},{32,0},{40,8},{48,16},{56,24},{1... | collective-permute-start | bytes 393224 | tf_op jit(solution)/shard_map/ppermute | solution.py:45
  161.9 10.5 %collective-permute-start.38 = (f32[2,2,8,1024]{3,2,1,0:T(8,128)S(1)}, f32[2,2,8,1024]{3,2,1,0:T(8,128)S(1)}, u32[]{:S(2)}, u32[]{:S(2)}) collective-permute-start(f32[2,2,8,1024]{3,2,1,0:T(8,128)S(1)} %slice.155), channel_id=1, source_target_pairs={{0,32},{8,40},{16,48},{24,56},{32,128},{40,136},{48,144},{56,152},... | collective-permute-start | bytes 393224 | tf_op jit(solution)/shard_map/ppermute | solution.py:46
  162.8 3.6 %collective-permute-start.41 = (f32[2,8,1]{1,2,0:T(1,128)S(1)}, f32[2,8,1]{1,2,0:T(1,128)S(1)}, u32[]{:S(2)}, u32[]{:S(2)}) collective-permute-start(f32[2,8,1]{1,2,0:T(1,128)S(1)} %pad_maximum_fusion.20), channel_id=1, source_target_pairs={{0,24},{8,0},{16,8},{24,16},{32,56},{40,32},{48,40},{56,48},{128,1... | collective-permute-start | bytes 200 | tf_op jit(solution)/shard_map/ppermute | solution.py:43
  162.8 4.9 %collective-permute-start.43 = (f32[2,8,1]{1,2,0:T(1,128)S(1)}, f32[2,8,1]{1,2,0:T(1,128)S(1)}, u32[]{:S(2)}, u32[]{:S(2)}) collective-permute-start(f32[2,8,1]{1,2,0:T(1,128)S(1)} %pad_maximum_fusion.20), channel_id=1, source_target_pairs={{0,8},{8,16},{16,24},{24,0},{32,40},{40,48},{48,56},{56,32},{128,1... | collective-permute-start | bytes 200 | tf_op jit(solution)/shard_map/ppermute | solution.py:42
  166.4 3.6 %collective-permute-start.42 = (f32[1,8,1]{1,2,0:T(1,128)S(1)}, f32[1,8,1]{1,2,0:T(1,128)S(1)}, u32[]{:S(2)}, u32[]{:S(2)}) collective-permute-start(f32[1,8,1]{1,2,0:T(1,128)S(1)} %slice.156), channel_id=1, source_target_pairs={{0,24},{8,0},{16,8},{24,16},{32,56},{40,32},{48,40},{56,48},{128,1... | collective-permute-start | bytes 104 | tf_op jit(solution)/shard_map/ppermute | solution.py:45
  167.7 4.8 %collective-permute-start.44 = (f32[1,8,1]{1,2,0:T(1,128)S(1)}, f32[1,8,1]{1,2,0:T(1,128)S(1)}, u32[]{:S(2)}, u32[]{:S(2)}) collective-permute-start(f32[1,8,1]{1,2,0:T(1,128)S(1)} %slice.157), channel_id=1, source_target_pairs={{0,8},{8,16},{16,24},{24,0},{32,40},{40,48},{48,56},{56,32},{128,1... | collective-permute-start | bytes 104 | tf_op jit(solution)/shard_map/ppermute | solution.py:46
  172.6 15.2 %collective-permute-start.39 = (f32[4,4,2,8,1024]{4,3,2,1,0:T(8,128)S(1)}, f32[4,4,2,8,1024]{4,3,2,1,0:T(8,128)}, u32[]{:S(2)}, u32[]{:S(2)}) collective-permute-start(f32[4,4,2,8,1024]{4,3,2,1,0:T(8,128)S(1)} %pad_maximum_fusion.3), channel_id=1, source_target_pairs={{0,64},{8,72},{16,80},{24,88},{32,96},{40,104},{48,112},{56,120},{... | collective-permute-start | bytes 3145736 | tf_op jit(solution)/shard_map/ppermute | solution.py:68
  172.7 3.8 %collective-permute-start.45 = (f32[4,2,8,1]{2,1,3,0:T(2,128)S(1)}, f32[4,2,8,1]{2,1,3,0:T(2,128)S(1)}, u32[]{:S(2)}, u32[]{:S(2)}) collective-permute-start(f32[4,2,8,1]{2,1,3,0:T(2,128)S(1)} %pad_maximum_fusion.19), channel_id=1, source_target_pairs={{0,160},{8,168},{16,176},{24,184},{32,0},{40,8},{48,16},{56,24},{1... | collective-permute-start | bytes 776 | tf_op jit(solution)/shard_map/ppermute | solution.py:43
  175.2 4.8 %collective-permute-start.47 = (f32[4,2,8,1]{2,1,3,0:T(2,128)S(1)}, f32[4,2,8,1]{2,1,3,0:T(2,128)S(1)}, u32[]{:S(2)}, u32[]{:S(2)}) collective-permute-start(f32[4,2,8,1]{2,1,3,0:T(2,128)S(1)} %pad_maximum_fusion.19), channel_id=1, source_target_pairs={{0,32},{8,40},{16,48},{24,56},{32,128},{40,136},{48,144},{56,152},... | collective-permute-start | bytes 776 | tf_op jit(solution)/shard_map/ppermute | solution.py:42
  176.5 4.8 %collective-permute-start.46 = (f32[2,2,8,1]{2,1,3,0:T(2,128)S(1)}, f32[2,2,8,1]{2,1,3,0:T(2,128)S(1)}, u32[]{:S(2)}, u32[]{:S(2)}) collective-permute-start(f32[2,2,8,1]{2,1,3,0:T(2,128)S(1)} %slice.158), channel_id=1, source_target_pairs={{0,160},{8,168},{16,176},{24,184},{32,0},{40,8},{48,16},{56,24},{1... | collective-permute-start | bytes 392 | tf_op jit(solution)/shard_map/ppermute | solution.py:45
  180.0 4.8 %collective-permute-start.48 = (f32[2,2,8,1]{2,1,3,0:T(2,128)S(1)}, f32[2,2,8,1]{2,1,3,0:T(2,128)S(1)}, u32[]{:S(2)}, u32[]{:S(2)}) collective-permute-start(f32[2,2,8,1]{2,1,3,0:T(2,128)S(1)} %slice.159), channel_id=1, source_target_pairs={{0,32},{8,40},{16,48},{24,56},{32,128},{40,136},{48,144},{56,152},... | collective-permute-start | bytes 392 | tf_op jit(solution)/shard_map/ppermute | solution.py:46
  205.5 4.3 %collective-permute-start.51 = (f32[2,8,1024]{2,1,0:T(8,128)S(1)}, f32[2,8,1024]{2,1,0:T(8,128)S(1)}, u32[]{:S(2)}, u32[]{:S(2)}) collective-permute-start(f32[2,8,1024]{2,1,0:T(8,128)S(1)} %get-tuple-element.56), channel_id=1, source_target_pairs={{0,24},{8,0},{16,8},{24,16},{32,56},{40,32},{48,40},{56,48},{128,1... | collective-permute-start | bytes 196616 | tf_op jit(solution)/shard_map/ppermute | solution.py:43
  205.6 5.6 %collective-permute-start.53 = (f32[2,8,1024]{2,1,0:T(8,128)S(1)}, f32[2,8,1024]{2,1,0:T(8,128)S(1)}, u32[]{:S(2)}, u32[]{:S(2)}) collective-permute-start(f32[2,8,1024]{2,1,0:T(8,128)S(1)} %get-tuple-element.56), channel_id=1, source_target_pairs={{0,8},{8,16},{16,24},{24,0},{32,40},{40,48},{48,56},{56,32},{128,1... | collective-permute-start | bytes 196616 | tf_op jit(solution)/shard_map/ppermute | solution.py:42
  209.8 3.9 %collective-permute-start.52 = (f32[1,8,1024]{2,1,0:T(8,128)S(1)}, f32[1,8,1024]{2,1,0:T(8,128)S(1)}, u32[]{:S(2)}, u32[]{:S(2)}) collective-permute-start(f32[1,8,1024]{2,1,0:T(8,128)S(1)} %slice.160), channel_id=1, source_target_pairs={{0,24},{8,0},{16,8},{24,16},{32,56},{40,32},{48,40},{56,48},{128,1... | collective-permute-start | bytes 98312 | tf_op jit(solution)/shard_map/ppermute | solution.py:45
  211.1 5.1 %collective-permute-start.54 = (f32[1,8,1024]{2,1,0:T(8,128)S(1)}, f32[1,8,1024]{2,1,0:T(8,128)S(1)}, u32[]{:S(2)}, u32[]{:S(2)}) collective-permute-start(f32[1,8,1024]{2,1,0:T(8,128)S(1)} %slice.161), channel_id=1, source_target_pairs={{0,8},{8,16},{16,24},{24,0},{32,40},{40,48},{48,56},{56,32},{128,1... | collective-permute-start | bytes 98312 | tf_op jit(solution)/shard_map/ppermute | solution.py:46
  216.3 6.4 %collective-permute-start.55 = (f32[4,2,8,1024]{3,2,1,0:T(8,128)S(1)}, f32[4,2,8,1024]{3,2,1,0:T(8,128)S(1)}, u32[]{:S(2)}, u32[]{:S(2)}) collective-permute-start(f32[4,2,8,1024]{3,2,1,0:T(8,128)S(1)} %get-tuple-element.32), channel_id=1, source_target_pairs={{0,160},{8,168},{16,176},{24,184},{32,0},{40,8},{48,16},{56,24},{1... | collective-permute-start | bytes 786440 | tf_op jit(solution)/shard_map/ppermute | solution.py:43
  216.4 7.7 %collective-permute-start.57 = (f32[4,2,8,1024]{3,2,1,0:T(8,128)S(1)}, f32[4,2,8,1024]{3,2,1,0:T(8,128)S(1)}, u32[]{:S(2)}, u32[]{:S(2)}) collective-permute-start(f32[4,2,8,1024]{3,2,1,0:T(8,128)S(1)} %get-tuple-element.32), channel_id=1, source_target_pairs={{0,32},{8,40},{16,48},{24,56},{32,128},{40,136},{48,144},{56,152},... | collective-permute-start | bytes 786440 | tf_op jit(solution)/shard_map/ppermute | solution.py:42
  222.8 5.0 %collective-permute-start.56 = (f32[2,2,8,1024]{3,2,1,0:T(8,128)S(1)}, f32[2,2,8,1024]{3,2,1,0:T(8,128)S(1)}, u32[]{:S(2)}, u32[]{:S(2)}) collective-permute-start(f32[2,2,8,1024]{3,2,1,0:T(8,128)S(1)} %slice.162), channel_id=1, source_target_pairs={{0,160},{8,168},{16,176},{24,184},{32,0},{40,8},{48,16},{56,24},{1... | collective-permute-start | bytes 393224 | tf_op jit(solution)/shard_map/ppermute | solution.py:45
  224.1 6.4 %collective-permute-start.58 = (f32[2,2,8,1024]{3,2,1,0:T(8,128)S(1)}, f32[2,2,8,1024]{3,2,1,0:T(8,128)S(1)}, u32[]{:S(2)}, u32[]{:S(2)}) collective-permute-start(f32[2,2,8,1024]{3,2,1,0:T(8,128)S(1)} %slice.163), channel_id=1, source_target_pairs={{0,32},{8,40},{16,48},{24,56},{32,128},{40,136},{48,144},{56,152},... | collective-permute-start | bytes 393224 | tf_op jit(solution)/shard_map/ppermute | solution.py:46
  230.6 2.7 collective-permute-start.59
  249.6 4.3 %collective-permute-start.61 = (f32[2,8,1024]{2,1,0:T(8,128)S(1)}, f32[2,8,1024]{2,1,0:T(8,128)S(1)}, u32[]{:S(2)}, u32[]{:S(2)}) collective-permute-start(f32[2,8,1024]{2,1,0:T(8,128)S(1)} %get-tuple-element.54), channel_id=1, source_target_pairs={{0,24},{8,0},{16,8},{24,16},{32,56},{40,32},{48,40},{56,48},{128,1... | collective-permute-start | bytes 196616 | tf_op jit(solution)/shard_map/ppermute | solution.py:43
  249.7 5.6 %collective-permute-start.63 = (f32[2,8,1024]{2,1,0:T(8,128)S(1)}, f32[2,8,1024]{2,1,0:T(8,128)S(1)}, u32[]{:S(2)}, u32[]{:S(2)}) collective-permute-start(f32[2,8,1024]{2,1,0:T(8,128)S(1)} %get-tuple-element.54), channel_id=1, source_target_pairs={{0,8},{8,16},{16,24},{24,0},{32,40},{40,48},{48,56},{56,32},{128,1... | collective-permute-start | bytes 196616 | tf_op jit(solution)/shard_map/ppermute | solution.py:42
  254.0 3.9 %collective-permute-start.62 = (f32[1,8,1024]{2,1,0:T(8,128)S(1)}, f32[1,8,1024]{2,1,0:T(8,128)S(1)}, u32[]{:S(2)}, u32[]{:S(2)}) collective-permute-start(f32[1,8,1024]{2,1,0:T(8,128)S(1)} %slice.164), channel_id=1, source_target_pairs={{0,24},{8,0},{16,8},{24,16},{32,56},{40,32},{48,40},{56,48},{128,1... | collective-permute-start | bytes 98312 | tf_op jit(solution)/shard_map/ppermute | solution.py:45
  255.3 5.1 %collective-permute-start.64 = (f32[1,8,1024]{2,1,0:T(8,128)S(1)}, f32[1,8,1024]{2,1,0:T(8,128)S(1)}, u32[]{:S(2)}, u32[]{:S(2)}) collective-permute-start(f32[1,8,1024]{2,1,0:T(8,128)S(1)} %slice.165), channel_id=1, source_target_pairs={{0,8},{8,16},{16,24},{24,0},{32,40},{40,48},{48,56},{56,32},{128,1... | collective-permute-start | bytes 98312 | tf_op jit(solution)/shard_map/ppermute | solution.py:46
  260.5 6.4 %collective-permute-start.65 = (f32[4,2,8,1024]{3,2,1,0:T(8,128)S(1)}, f32[4,2,8,1024]{3,2,1,0:T(8,128)S(1)}, u32[]{:S(2)}, u32[]{:S(2)}) collective-permute-start(f32[4,2,8,1024]{3,2,1,0:T(8,128)S(1)} %get-tuple-element.30), channel_id=1, source_target_pairs={{0,160},{8,168},{16,176},{24,184},{32,0},{40,8},{48,16},{56,24},{1... | collective-permute-start | bytes 786440 | tf_op jit(solution)/shard_map/ppermute | solution.py:43
  260.6 7.7 %collective-permute-start.67 = (f32[4,2,8,1024]{3,2,1,0:T(8,128)S(1)}, f32[4,2,8,1024]{3,2,1,0:T(8,128)S(1)}, u32[]{:S(2)}, u32[]{:S(2)}) collective-permute-start(f32[4,2,8,1024]{3,2,1,0:T(8,128)S(1)} %get-tuple-element.30), channel_id=1, source_target_pairs={{0,32},{8,40},{16,48},{24,56},{32,128},{40,136},{48,144},{56,152},... | collective-permute-start | bytes 786440 | tf_op jit(solution)/shard_map/ppermute | solution.py:42
  266.9 5.0 %collective-permute-start.66 = (f32[2,2,8,1024]{3,2,1,0:T(8,128)S(1)}, f32[2,2,8,1024]{3,2,1,0:T(8,128)S(1)}, u32[]{:S(2)}, u32[]{:S(2)}) collective-permute-start(f32[2,2,8,1024]{3,2,1,0:T(8,128)S(1)} %slice.166), channel_id=1, source_target_pairs={{0,160},{8,168},{16,176},{24,184},{32,0},{40,8},{48,16},{56,24},{1... | collective-permute-start | bytes 393224 | tf_op jit(solution)/shard_map/ppermute | solution.py:45
  268.3 6.5 %collective-permute-start.68 = (f32[2,2,8,1024]{3,2,1,0:T(8,128)S(1)}, f32[2,2,8,1024]{3,2,1,0:T(8,128)S(1)}, u32[]{:S(2)}, u32[]{:S(2)}) collective-permute-start(f32[2,2,8,1024]{3,2,1,0:T(8,128)S(1)} %slice.167), channel_id=1, source_target_pairs={{0,32},{8,40},{16,48},{24,56},{32,128},{40,136},{48,144},{56,152},... | collective-permute-start | bytes 393224 | tf_op jit(solution)/shard_map/ppermute | solution.py:46
  274.8 2.7 collective-permute-start.69
  293.8 3.6 %collective-permute-start.71 = (f32[16]{0:T(128)S(1)}, f32[16]{0:T(128)S(1)}, u32[]{:S(2)}, u32[]{:S(2)}) collective-permute-start(f32[16]{0:T(128)S(1)} %add.557), channel_id=1, source_target_pairs={{0,32},{8,40},{16,48},{24,56},{32,0},{40,8},{48,16},{56,24},{128,1... | collective-permute-start | bytes 200 | tf_op jit(solution)/shard_map/ppermute | solution.py:109
  297.4 3.6 %collective-permute-start.72 = (f32[16]{0:T(128)S(1)}, f32[16]{0:T(128)S(1)}, u32[]{:S(2)}, u32[]{:S(2)}) collective-permute-start(f32[16]{0:T(128)S(1)} %add.558), channel_id=1, source_target_pairs={{0,8},{8,0},{16,24},{24,16},{32,40},{40,32},{48,56},{56,48},{128,1... | collective-permute-start | bytes 200 | tf_op jit(solution)/shard_map/ppermute | solution.py:109
  301.0 5.1 %collective-permute-start.73 = (f32[16]{0:T(128)S(1)}, f32[16]{0:T(128)S(1)}, u32[]{:S(2)}, u32[]{:S(2)}) collective-permute-start(f32[16]{0:T(128)S(1)} %add.559), channel_id=1, source_target_pairs={{0,128},{8,136},{16,144},{24,152},{32,160},{40,168},{48,176},{56,1... | collective-permute-start | bytes 200 | tf_op jit(solution)/shard_map/ppermute | solution.py:109
  306.0 5.1 %collective-permute-start.74 = (f32[16]{0:T(128)S(1)}, f32[16]{0:T(128)S(1)}, u32[]{:S(2)}, u32[]{:S(2)}) collective-permute-start(f32[16]{0:T(128)S(1)} %add.560), channel_id=1, source_target_pairs={{0,16},{8,24},{16,0},{24,8},{32,48},{40,56},{48,32},{56,40},{128,1... | collective-permute-start | bytes 200 | tf_op jit(solution)/shard_map/ppermute | solution.py:109
  (12 other events, 33.5 us)
